TPU v7x, 32 devices: a whole 2x2x4 slice. The times are simulated.
32 devices in a mesh: row: 4 (over z), col: 8 (over y, x, core).
Axes of the slice: x: 2, y: 2, z: 4, core: 2. Of those that a mesh axis runs over, the one named last changes fastest.
Arguments:
- factor_rows: float32 [2, 1024, 4096], P(None, 'col', 'row'), as said below
- adjoint_rows: float32 [2, 1024, 4096], P(None, 'col', 'row'), as said below
- panel_inverse: float32 [2, 1024, 1024], replicated, as said below
Outputs:
- kernel_adjoint: float32 [2, 1024, 4096], P(None, 'col', 'row')
Inputs may be any that keep to these rules, and one draw needn't show every extreme that they name: `factor_rows`: zero right of the diagonal; in panel p the columns J_p hold a lower-triangular block with diagonal entries from 0.5 to 4. `adjoint_rows`: zero right of the diagonal of the same rows. panel_inverse[p] is the inverse of factor_rows[p, :, J_p] to float32 rounding.
All inputs are finite; a program needn't handle non-finite values.
Results may differ from a plain program's by a relative error of at most 0.0001.
Values sent between devices are 32-bit elements; how exact they have to be, the bound alone decides.
No kernel may reach another device: no remote copies, remote signals or barrier semaphores. Data moves between devices by JAX's collectives and lax.ppermute only.
A program may use at most 128 MiB of HBM per device.

v0:
```python
import jax
import jax.numpy as jnp
from jax import lax
from jax.sharding import PartitionSpec as P
from jax.experimental import pallas as pl
from jax.experimental.pallas import tpu as pltpu

PRECISION = lax.Precision.HIGH


def mm(left, right):
    return jnp.dot(left, right, precision=PRECISION, preferred_element_type=jnp.float32)


def tmm(left, right):
    return lax.dot_general(left, right, (((0,), (0,)), ((), ())), precision=PRECISION,
                           preferred_element_type=jnp.float32)


def phi(matrix):
    eye = jnp.eye(matrix.shape[0], dtype=jnp.float32)
    return jnp.tril(matrix) * (1.0 - 0.5 * eye)


def sandwich_half(lower_half, inverse):
    return tmm(inverse, mm(lower_half, inverse))


def _sym_kernel(flag_ref, u_ref, ut_ref, alt_ref, o_ref):
    o_ref[...] = jnp.where(flag_ref[0] != 0, u_ref[...] + ut_ref[...].T, alt_ref[...])


def sym_select(flag, half, other, block=256):
    count = half.shape[0] // block
    spec = pl.BlockSpec((block, block), lambda i, j, f: (i, j))
    spec_t = pl.BlockSpec((block, block), lambda i, j, f: (j, i))
    return pl.pallas_call(
        _sym_kernel,
        grid_spec=pltpu.PrefetchScalarGridSpec(
            num_scalar_prefetch=1, grid=(count, count),
            in_specs=[spec, spec_t, spec], out_specs=spec),
        out_shape=jax.ShapeDtypeStruct(half.shape, half.dtype),
    )(jnp.reshape(flag.astype(jnp.int32), (1,)), half, half, other)


def row_bcast(value, source, targets):
    row = lax.axis_index("row")
    recv = None
    for target in targets:
        got = lax.ppermute(value, "row", [(source, target)])
        recv = got if recv is None else recv + got
    if recv is None:
        return value
    return jnp.where(row == source, value, recv)


def local(factor_rows, adjoint_rows, panel_inverse):
    row_count = lax.axis_size("row")
    panels = panel_inverse.shape[0]
    width = panel_inverse.shape[1]
    slab = factor_rows.shape[1]
    assert panels == 2 and factor_rows.shape[2] == width
    row = lax.axis_index("row")
    offset = lax.axis_index("col") * slab
    own1 = row_count - 1
    own0 = row_count - 2

    grow = offset + jnp.arange(slab, dtype=jnp.int32)[:, None]
    gcol = jnp.arange(width, dtype=jnp.int32)[None, :]
    lower = gcol <= grow
    diag_scale = jnp.where(gcol == grow, 0.5, 1.0).astype(jnp.float32)

    f0, f1 = factor_rows[0], factor_rows[1]
    a0, a1 = adjoint_rows[0], adjoint_rows[1]
    inv0, inv1 = panel_inverse[0], panel_inverse[1]

    full1 = lax.all_gather(f1, "col", axis=0, tiled=True)
    half1 = sandwich_half(phi(tmm(f1, jnp.where(lower, a1, 0.0))), inv1)
    part1 = sym_select(jnp.array(True), half1, half1)
    full1, part1 = lax.optimization_barrier((full1, part1))
    v1 = lax.psum_scatter(part1, "col", scatter_dimension=0, tiled=True)
    diag1 = jnp.where(lower, v1, 0.0) * diag_scale
    f0_in, v1 = lax.optimization_barrier((f0, v1))
    full0 = lax.all_gather(f0_in, "col", axis=0, tiled=True)
    v1_near = jnp.where(row == own1, v1, lax.ppermute(v1, "row", [(own1, own0)]))
    a1_left = a1 - mm(v1_near, full1)

    col_adj = mm(a1_left, inv0)
    forward = jnp.stack([v1_near, col_adj])
    received = [lax.ppermute(forward, "row", [(own0, target)]) for target in range(own0)]
    x0 = tmm(f0, jnp.where(lower, a0, 0.0)) - tmm(full0, jnp.tril(tmm(col_adj, f1)))
    part0 = sandwich_half(phi(x0), inv0)
    received, part0 = lax.optimization_barrier((received, part0))
    sent = sum(received[1:], received[0]) if received else forward
    cross = tmm(sent[1], f1)
    summed = lax.psum_scatter(sym_select(row == own0, part0, cross), "col",
                              scatter_dimension=0, tiled=True)
    diag0 = jnp.where(lower, summed, 0.0) * diag_scale
    v0 = row_bcast(summed, own0, list(range(own0)))

    left1 = a1 - mm(sent[0], full1) - mm(sent[1], full0)
    left0 = a0 - summed - mm(v0, full0)
    out1 = jnp.where(row < own0, left1, jnp.where(row == own0, col_adj, diag1))
    out0 = jnp.where(row < own0, left0, jnp.where(row == own0, diag0, a0))
    return jnp.stack([out0, out1])


def solution(mesh):
    return jax.shard_map(
        local,
        mesh=mesh,
        in_specs=(P(None, "col", "row"), P(None, "col", "row"), P()),
        out_specs=P(None, "col", "row"),
        check_vma=False,
    )
```

profile of v0, /device:TPU:8, one launch (start us, length us, event | category | flops | bytes accessed | tf_op | source)
XLA Modules:
  0.0 277.5 jit_solution(7754515068276295903)
XLA Ops:
  6.5 2.3 slice_bitcast_fusion.3
  8.9 3.2 %fusion.45 = f32[1024,1024]{0,1:T(8,128)S(1)} fusion(f32[2,128,1024]{2,1,0:T(8,128)} %param.4, s32[128]{0:T(128)S(1)} %iota_add_fusion, f32[2,128,1024]{2,1,0:T(8,128)} %param.3), kind=kOutput, calls=%fused_computation.54 | convolution fusion | flops 805568512 | bytes 5243392 | tf_op jit(solution)/shard_map/dot_general | solution.py:16
  12.2 9.3 %fusion.11 = f32[1024,1024]{1,0:T(8,128)S(1)} fusion(f32[1024,1024]{0,1:T(8,128)S(1)} %fusion.45, f32[2,1024,1024]{2,1,0:T(8,128)} %param.5), kind=kOutput, calls=%fused_computation.11 | convolution fusion | flops 6448742400 | bytes 12582912 | tf_op jit(solution)/shard_map/dot_general | solution.py:12
  21.5 8.3 %fusion.22.u_ref.ut_ref.alt_ref = f32[1024,1024]{1,0:T(8,128)} fusion(f32[1024,1024]{1,0:T(8,128)S(1)} %fusion.11, f32[2,1024,1024]{2,1,0:T(8,128)S(1)} %bitcast.85), kind=kOutput, calls=%fused_computation.25 | convolution fusion | flops 6442450944 | bytes 12582912 | tf_op jit(solution)/shard_map/dot_general | solution.py:16
  29.9 12.9 %shard_map.37 = f32[1024,1024]{1,0:T(8,128)} custom-call(s32[1]{0:T(128)} %constant.12.clone.1.flag_ref, f32[1024,1024]{1,0:T(8,128)} %fusion.22.u_ref.ut_ref.alt_ref, f32[1024,1024]{1,0:T(8,128)} %fusion.22.u_ref.ut_ref.alt_ref, f32[1024,1024]{1,0:T(8,128)} %fusion.22.u_ref.ut_ref.alt_ref), custom_call_target="tpu_custom_call" | custom-call | tf_op jit(solution)/shard_map/pallas_call | solution.py:37
  42.8 4.4 %all-gather.6.cloned.1.call-done = f32[1,1024,1024]{2,1,0:T(8,128)} async-done(((f32[1,128,1024]{2,1,0:T(8,128)}), f32[1,1024,1024]{2,1,0:T(8,128)}) %all-gather.6.cloned.1.call-update) | async-done | bytes 4194320 | tf_op jit(solution)/shard_map/all_gather | solution.py:77
  47.2 54.7 %reduce-scatter.3.cloned.1.call-done = f32[128,1024]{1,0:T(8,128)} async-done(((f32[1024,1024]{1,0:T(8,128)}), f32[128,1024]{1,0:T(8,128)}) %reduce-scatter.3.cloned.1.call-update) | async-done | bytes 524304 | tf_op jit(solution)/shard_map/reduce_scatter | solution.py:81
  103.0 3.9 %fusion.41 = f32[1024,1024]{0,1:T(8,128)} fusion(f32[2,128,1024]{2,1,0:T(8,128)S(1)} %copy-done.3, s32[128]{0:T(128)S(1)} %iota_add_fusion, f32[2,128,1024]{2,1,0:T(8,128)S(1)} %copy-done.2), kind=kOutput, calls=%fused_computation.50 | convolution fusion | flops 805568512 | bytes 5243392 | tf_op jit(solution)/shard_map/dot_general | solution.py:16
  107.0 1.6 convolution_subtract_fusion.3
  108.6 3.6 %fusion.7 = f32[128,1024]{1,0:T(8,128)S(1)} fusion(f32[128,1024]{1,0:T(8,128)S(1)} %convolution_subtract_fusion.3, f32[2,1024,1024]{2,1,0:T(8,128)} %param.5), kind=kOutput, calls=%fused_computation.7 | convolution fusion | flops 805306368 | bytes 5242880 | tf_op jit(solution)/shard_map/dot_general | solution.py:12
  115.3 3.8 %fusion.43 = f32[1024,1024]{1,0:T(8,128)} fusion(f32[128,1024]{1,0:T(8,128)S(1)} %fusion.7, f32[2,128,1024]{2,1,0:T(8,128)S(1)} %copy-done.2), kind=kOutput, calls=%fused_computation.52 | convolution fusion | flops 805306368 | bytes 5242880 | tf_op jit(solution)/shard_map/dot_general | solution.py:16
  119.1 21.6 %all-gather.4.cloned.1.call-done = f32[1024,1024]{1,0:T(8,128)} async-done(((f32[128,1024]{1,0:T(8,128)}), f32[1024,1024]{1,0:T(8,128)}) %all-gather.4.cloned.1.call-update) | async-done | bytes 4194320 | tf_op jit(solution)/shard_map/all_gather | solution.py:84
  140.7 10.4 %fusion.15 = f32[1024,1024]{1,0:T(8,128)S(1)} fusion(f32[1024,1024]{1,0:T(8,128)} %all-gather.4.cloned.1.call-done, f32[1024,1024]{1,0:T(8,128)} %fusion.43), kind=kOutput, calls=%fused_computation.15 | convolution fusion | flops 6444548096 | bytes 12582912 | tf_op jit(solution)/shard_map/dot_general | solution.py:16
  151.1 9.3 %fusion.2 = f32[1024,1024]{1,0:T(8,128)S(1)} fusion(f32[1024,1024]{1,0:T(8,128)S(1)} %fusion.15, f32[1024,1024]{0,1:T(8,128)S(1)} %copy-done.6, f32[2,1024,1024]{2,1,0:T(8,128)} %param.5), kind=kOutput, calls=%fused_computation.3 | convolution fusion | flops 6449790976 | bytes 16777216 | tf_op jit(solution)/shard_map/dot_general | solution.py:12
  160.4 10.0 %fusion.25.u_ref.ut_ref = f32[1024,1024]{1,0:T(8,128)} fusion(f32[1024,1024]{1,0:T(8,128)S(1)} %fusion.2, f32[2,1024,1024]{2,1,0:T(8,128)} %param.5), kind=kOutput, calls=%fused_computation.26 | convolution fusion | flops 6442450944 | bytes 12582912 | tf_op jit(solution)/shard_map/dot_general | solution.py:16
  172.1 1.7 add.23
  173.8 3.8 %fusion.47.alt_ref = f32[1024,1024]{1,0:T(8,128)} fusion(f32[2,128,1024]{2,1,0:T(8,128)S(1)} %add.23, f32[2,128,1024]{2,1,0:T(8,128)S(1)} %copy-done.2), kind=kOutput, calls=%fused_computation.56 | convolution fusion | flops 805306368 | bytes 5242880 | tf_op jit(solution)/shard_map/dot_general | solution.py:16
  177.6 12.6 %shard_map.38 = f32[1024,1024]{1,0:T(8,128)} custom-call(s32[1]{0:T(128)} %bitcast.1.flag_ref, f32[1024,1024]{1,0:T(8,128)} %fusion.25.u_ref.ut_ref, f32[1024,1024]{1,0:T(8,128)} %fusion.25.u_ref.ut_ref, f32[1024,1024]{1,0:T(8,128)} %fusion.47.alt_ref), custom_call_target="tpu_custom_call" | custom-call | tf_op jit(solution)/shard_map/pallas_call | solution.py:37
  190.2 50.9 %reduce-scatter.5.cloned.1.call-done = f32[128,1024]{1,0:T(8,128)} async-done(((f32[1024,1024]{1,0:T(8,128)}), f32[128,1024]{1,0:T(8,128)}) %reduce-scatter.5.cloned.1.call-update) | async-done | bytes 524304 | tf_op jit(solution)/shard_map/reduce_scatter | solution.py:96
  241.9 1.4 collective-permute-start.4
  243.3 3.6 %convolution_subtract_fusion.1 = f32[128,1024]{1,0:T(8,128)S(1)} fusion(f32[1024,1024]{1,0:T(8,128)} %bitcast.81, f32[2,128,1024]{2,1,0:T(8,128)S(1)} %add.23, f32[2,128,1024]{2,1,0:T(8,128)S(1)} %copy-done.4), kind=kOutput, calls=%fused_computation.37 | convolution fusion | flops 805437440 | bytes 5767168 | tf_op jit(solution)/shard_map/dot_general | solution.py:12
  246.9 1.7 fusion.36
  248.6 19.7 %collective-permute-done.4 = f32[128,1024]{1,0:T(8,128)S(1)} collective-permute-done((f32[128,1024]{1,0:T(8,128)}, f32[128,1024]{1,0:T(8,128)S(1)}, u32[]{:S(2)}, u32[]{:S(2)}) %collective-permute-start.4) | collective-permute-done | bytes 524320 | tf_op jit(solution)/shard_map/ppermute | solution.py:50
  268.3 1.6 fusion.38
  (43 shorter events, 7.9 us)
Async XLA Ops:
  6.5 40.6 %all-gather.6.cloned.1.call-start = ((), (), s32[]{:S(2)}) async-start(), calls=%async_computation.5 | async-start | bytes 4718592 | tf_op jit(solution)/shard_map/all_gather | solution.py:77
  8.8 93.1 %reduce-scatter.3.cloned.1.call-start = ((), (), s32[]{:S(2)}) async-start(), calls=%async_computation.2 | async-start | bytes 4718592 | tf_op jit(solution)/shard_map/reduce_scatter | solution.py:81
  8.9 12.6 %slice-start = ((s8[8388608]{0:T(1024)(128)(4,1)}), s8[4194304]{0:T(1024)(128)(4,1)S(1)}, s32[]{:S(2)}) async-start(s8[8388608]{0:T(1024)(128)(4,1)} %bitcast.84), calls=%async_computation.6 | async-start | bytes 8388608
  12.2 9.3 %slice-start.1 = ((s8[8388608]{0:T(1024)(128)(4,1)}), s8[4194304]{0:T(1024)(128)(4,1)S(1)}, s32[]{:S(2)}) async-start(s8[8388608]{0:T(1024)(128)(4,1)} %bitcast.84), calls=%async_computation.7 | async-start | bytes 8388608
  42.8 60.2 %copy-start.2 = (f32[2,128,1024]{2,1,0:T(8,128)S(1)}, f32[2,128,1024]{2,1,0:T(8,128)}, u32[]{:S(2)}) copy-start(f32[2,128,1024]{2,1,0:T(8,128)} %param.3) | copy-start | bytes 3145732
  42.8 60.2 %copy-start.3 = (f32[2,128,1024]{2,1,0:T(8,128)S(1)}, f32[2,128,1024]{2,1,0:T(8,128)}, u32[]{:S(2)}) copy-start(f32[2,128,1024]{2,1,0:T(8,128)} %param.4) | copy-start | bytes 3145732
  47.2 93.5 %all-gather.4.cloned.1.call-start = ((), (), s32[]{:S(2)}) async-start(), calls=%async_computation.3 | async-start | bytes 4718592 | tf_op jit(solution)/shard_map/all_gather | solution.py:84
  101.9 5.0 %copy-start.5 = (f32[128,1024]{1,0:T(8,128)S(1)}, f32[128,1024]{1,0:T(8,128)}, u32[]{:S(2)}) copy-start(f32[128,1024]{1,0:T(8,128)} %reduce-scatter.3.cloned.1.call-done) | copy-start | bytes 1572868
  101.9 139.1 %reduce-scatter.5.cloned.1.call-start = ((), (), s32[]{:S(2)}) async-start(), calls=%async_computation.4 | async-start | bytes 4718592 | tf_op jit(solution)/shard_map/reduce_scatter | solution.py:96
  102.0 4.9 %collective-permute-start = (f32[128,1024]{1,0:T(8,128)}, f32[128,1024]{1,0:T(8,128)S(1)}, u32[]{:S(2)}, u32[]{:S(2)}) collective-permute-start(f32[128,1024]{1,0:T(8,128)} %reduce-scatter.3.cloned.1.call-done), channel_id=1, source_target_pairs={{24,16},{25,17},{26,18},{27,19},{28,20},{29,21},{30,22},{31,23}} | collective-permute-start | bytes 1572872 | tf_op jit(solution)/shard_map/ppermute | solution.py:85
  103.0 4.0 %copy-start.1 = (f32[1,1024,1024]{2,1,0:T(8,128)S(1)}, f32[1,1024,1024]{2,1,0:T(8,128)}, u32[]{:S(2)}) copy-start(f32[1,1024,1024]{2,1,0:T(8,128)} %all-gather.6.cloned.1.call-done) | copy-start | bytes 12582916
  113.3 57.2 %collective-permute-start.1 = (f32[2,128,1024]{2,1,0:T(8,128)}, f32[2,128,1024]{2,1,0:T(8,128)S(1)}, u32[]{:S(2)}, u32[]{:S(2)}) collective-permute-start(f32[2,128,1024]{2,1,0:T(8,128)} %pad_maximum_fusion), channel_id=1, source_target_pairs={{16,0},{17,1},{18,2},{19,3},{20,4},{21,5},{22,6},{23,7}} | collective-permute-start | bytes 3145736 | tf_op jit(solution)/shard_map/ppermute | solution.py:90
  114.0 58.1 %collective-permute-start.2 = (f32[2,128,1024]{2,1,0:T(8,128)}, f32[2,128,1024]{2,1,0:T(8,128)}, u32[]{:S(2)}, u32[]{:S(2)}) collective-permute-start(f32[2,128,1024]{2,1,0:T(8,128)} %pad_maximum_fusion), channel_id=1, source_target_pairs={{16,8},{17,9},{18,10},{19,11},{20,12},{21,13},{22,14},{23,15}} | collective-permute-start | bytes 3145736 | tf_op jit(solution)/shard_map/ppermute | solution.py:90
  140.7 10.4 %copy-start.6 = (f32[1024,1024]{0,1:T(8,128)S(1)}, f32[1024,1024]{0,1:T(8,128)}, u32[]{:S(2)}) copy-start(f32[1024,1024]{0,1:T(8,128)} %fusion.41) | copy-start | bytes 12582916
  170.4 1.0 copy-start.7
  190.2 53.2 %copy-start.4 = (f32[2,128,1024]{2,1,0:T(8,128)S(1)}, f32[2,128,1024]{2,1,0:T(8,128)}, u32[]{:S(2)}) copy-start(f32[2,128,1024]{2,1,0:T(8,128)} %param.4) | copy-start | bytes 3145732
  241.1 5.8 %copy-start = (f32[1024,1024]{1,0:T(8,128)S(1)}, f32[1024,1024]{1,0:T(8,128)}, u32[]{:S(2)}) copy-start(f32[1024,1024]{1,0:T(8,128)} %all-gather.4.cloned.1.call-done) | copy-start | bytes 12582916
  241.1 7.6 %collective-permute-start.3 = (f32[128,1024]{1,0:T(8,128)}, f32[128,1024]{1,0:T(8,128)S(1)}, u32[]{:S(2)}, u32[]{:S(2)}) collective-permute-start(f32[128,1024]{1,0:T(8,128)} %reduce-scatter.5.cloned.1.call-done), channel_id=1, source_target_pairs={{16,0},{17,1},{18,2},{19,3},{20,4},{21,5},{22,6},{23,7}} | collective-permute-start | bytes 1572872 | tf_op jit(solution)/shard_map/ppermute | solution.py:50
  241.9 26.4 %collective-permute-start.4 = (f32[128,1024]{1,0:T(8,128)}, f32[128,1024]{1,0:T(8,128)S(1)}, u32[]{:S(2)}, u32[]{:S(2)}) collective-permute-start(f32[128,1024]{1,0:T(8,128)} %reduce-scatter.5.cloned.1.call-done), channel_id=1, source_target_pairs={{16,8},{17,9},{18,10},{19,11},{20,12},{21,13},{22,14},{23,15}} | collective-permute-start | bytes 1572872 | tf_op jit(solution)/shard_map/ppermute | solution.py:50
  246.9 21.4 %copy-start.8 = (f32[128,1024]{1,0:T(8,128)S(1)}, f32[128,1024]{1,0:T(8,128)}, u32[]{:S(2)}) copy-start(f32[128,1024]{1,0:T(8,128)} %reduce-scatter.5.cloned.1.call-done) | copy-start | bytes 1572868
Sparse Core Ops, SparseCore 0:
  9.2 37.8 all-gather.5
  50.5 51.3 reduce-scatter.2
  103.9 36.6 all-gather.3
  190.3 50.6 reduce-scatter.4
where the time goes:
time: 278 us
  waiting for transfers between devices  152 us (55%)
  matrix products  74.2 us (27%)
  Pallas kernels  25.5 us (9%)
  between operations  13.4 us (5%)
  starting transfers between devices  5.37 us (2%)
  other arithmetic  3.85 us (1%)
  local copies, waits for them, and re-layouts  3.36 us (1%)
    reduce_scatter x1, waiting for transfers between devices, local(): v1 = lax.psum_scatter(part1, 'col', scatter_dimension=0, tiled=True)  54.7 us
    reduce_scatter x1, waiting for transfers between devices, local(): lax.psum_scatter(sym_select(row == own0, part0, cross), 'col', scatter_di...  50.9 us
    dot_general x7, matrix products, tmm(): lax.dot_general(left, right, (((0,), (0,)), ((), ())), precision=PRECISIO...  43.5 us
    dot_general x7, matrix products, mm(): jnp.dot(left, right, precision=PRECISION, preferred_element_type=jnp.floa...  30.7 us
    pallas_call x2, Pallas kernels, sym_select(): pl.pallas_call(_sym_kernel, grid_spec=pltpu.PrefetchScalarGridSpec(num_sc...  25.5 us
    all_gather x1, waiting for transfers between devices, local(): full0 = lax.all_gather(f0_in, 'col', axis=0, tiled=True)  21.6 us
    ppermute x2, waiting for transfers between devices, row_bcast(): got = lax.ppermute(value, 'row', [(source, target)])  19.7 us
  transfers between devices with their start and end apart: 9, of which 6 were waited for; matrix products, arithmetic and copies ran while one was open for 25% of the time, Pallas kernels for 5%

commit v1 on v0

--- a/solution.py
+++ b/solution.py
@@ -30,16 +30,19 @@
     o_ref[...] = jnp.where(flag_ref[0] != 0, u_ref[...] + ut_ref[...].T, alt_ref[...])
 
 
-def sym_select(flag, half, other, block=256):
-    count = half.shape[0] // block
+def sym_select(flag, half, other, parts=1, block=256):
+    size = half.shape[0]
+    count = size // block
+    per_part = count // parts
     spec = pl.BlockSpec((block, block), lambda i, j, f: (i, j))
     spec_t = pl.BlockSpec((block, block), lambda i, j, f: (j, i))
+    out_spec = pl.BlockSpec((None, block, block), lambda i, j, f: (j // per_part, i, j % per_part))
     return pl.pallas_call(
         _sym_kernel,
         grid_spec=pltpu.PrefetchScalarGridSpec(
             num_scalar_prefetch=1, grid=(count, count),
-            in_specs=[spec, spec_t, spec], out_specs=spec),
-        out_shape=jax.ShapeDtypeStruct(half.shape, half.dtype),
+            in_specs=[spec, spec_t, spec], out_specs=out_spec),
+        out_shape=jax.ShapeDtypeStruct((parts, size, size // parts), half.dtype),
     )(jnp.reshape(flag.astype(jnp.int32), (1,)), half, half, other)
 
 
@@ -76,7 +79,7 @@
 
     full1 = lax.all_gather(f1, "col", axis=0, tiled=True)
     half1 = sandwich_half(phi(tmm(f1, jnp.where(lower, a1, 0.0))), inv1)
-    part1 = sym_select(jnp.array(True), half1, half1)
+    part1 = sym_select(jnp.array(True), half1, half1)[0]
     full1, part1 = lax.optimization_barrier((full1, part1))
     v1 = lax.psum_scatter(part1, "col", scatter_dimension=0, tiled=True)
     diag1 = jnp.where(lower, v1, 0.0) * diag_scale
@@ -93,13 +96,20 @@
     received, part0 = lax.optimization_barrier((received, part0))
     sent = sum(received[1:], received[0]) if received else forward
     cross = tmm(sent[1], f1)
-    summed = lax.psum_scatter(sym_select(row == own0, part0, cross), "col",
-                              scatter_dimension=0, tiled=True)
+    panels_in = sym_select(row == own0, part0, cross, parts=2)
+    summed = []
+    v0 = []
+    for piece in range(2):
+        got = lax.psum_scatter(panels_in[piece], "col", scatter_dimension=0, tiled=True)
+        summed.append(got)
+        v0.append(row_bcast(got, own0, list(range(own0))))
+    summed = jnp.concatenate(summed, axis=1)
     diag0 = jnp.where(lower, summed, 0.0) * diag_scale
-    v0 = row_bcast(summed, own0, list(range(own0)))
+    split = width // 2
+    v0_term = mm(v0[0], full0[:split]) + mm(v0[1], full0[split:])
 
     left1 = a1 - mm(sent[0], full1) - mm(sent[1], full0)
-    left0 = a0 - summed - mm(v0, full0)
+    left0 = a0 - summed - v0_term
     out1 = jnp.where(row < own0, left1, jnp.where(row == own0, col_adj, diag1))
     out0 = jnp.where(row < own0, left0, jnp.where(row == own0, diag0, a0))
     return jnp.stack([out0, out1])

time: 278 us -> 306 us (1.10)
  the two profiles are of different devices: /device:TPU:8 before, /device:TPU:0 now
where the time goes in v1:
time: 306 us; the launch traced here: 303 us
  waiting for transfers between devices  161 us (53%)
  matrix products  79.8 us (26%)
  Pallas kernels  25.5 us (8%)
  between operations  13.4 us (4%)
  local copies, waits for them, and re-layouts  9.59 us (3%)
  starting transfers between devices  9.12 us (3%)
  other arithmetic  3.87 us (1%)
    reduce_scatter x2, waiting for transfers between devices, local(): lax.psum_scatter(panels_in[piece], 'col', scatter_dimension=0, tiled=True)  73 us
    reduce_scatter x1, waiting for transfers between devices, local(): v1 = lax.psum_scatter(part1, 'col', scatter_dimension=0, tiled=True)  54.7 us
    dot_general x7, matrix products, tmm(): lax.dot_general(left, right, (((0,), (0,)), ((), ())), precision=PRECISIO...  43.6 us
    dot_general x8, matrix products, mm(): jnp.dot(left, right, precision=PRECISION, preferred_element_type=jnp.floa...  36.3 us
    pallas_call x2, Pallas kernels, sym_select(): pl.pallas_call(_sym_kernel, grid_spec=pltpu.PrefetchScalarGridSpec(num_sc...  25.5 us
    all_gather x1, waiting for transfers between devices, local(): full0 = lax.all_gather(f0_in, 'col', axis=0, tiled=True)  20.6 us
    ppermute x4, waiting for transfers between devices, row_bcast(): got = lax.ppermute(value, 'row', [(source, target)])  6.63 us
  transfers between devices with their start and end apart: 12, of which 6 were waited for; matrix products, arithmetic and copies ran while one was open for 25% of the time, Pallas kernels for 4%

profile of v1, /device:TPU:0, one launch (start us, length us, event | category | flops | bytes accessed | tf_op | source)
XLA Modules:
  0.0 302.6 jit_solution(3224085717860751707)
XLA Ops:
  6.5 2.3 slice_bitcast_fusion.5
  8.9 3.2 %fusion.59 = f32[1024,1024]{0,1:T(8,128)S(1)} fusion(f32[2,128,1024]{2,1,0:T(8,128)} %param.4, s32[128]{0:T(128)S(1)} %iota_add_fusion, f32[2,128,1024]{2,1,0:T(8,128)} %param.3), kind=kOutput, calls=%fused_computation.61 | convolution fusion | flops 805568512 | bytes 5243392 | tf_op jit(solution)/shard_map/dot_general | solution.py:16
  12.2 9.3 %fusion.11 = f32[1024,1024]{1,0:T(8,128)S(1)} fusion(f32[1024,1024]{0,1:T(8,128)S(1)} %fusion.59, f32[2,1024,1024]{2,1,0:T(8,128)} %param.5), kind=kOutput, calls=%fused_computation.11 | convolution fusion | flops 6448742400 | bytes 12582912 | tf_op jit(solution)/shard_map/dot_general | solution.py:12
  21.5 8.4 %fusion.22.u_ref.ut_ref.alt_ref = f32[1024,1024]{1,0:T(8,128)} fusion(f32[1024,1024]{1,0:T(8,128)S(1)} %fusion.11, f32[2,1024,1024]{2,1,0:T(8,128)S(1)} %bitcast.90), kind=kOutput, calls=%fused_computation.25 | convolution fusion | flops 6442450944 | bytes 12582912 | tf_op jit(solution)/shard_map/dot_general | solution.py:16
  29.9 12.9 %shard_map.37 = f32[1,1024,1024]{2,1,0:T(8,128)} custom-call(s32[1]{0:T(128)} %constant.12.clone.1.flag_ref, f32[1024,1024]{1,0:T(8,128)} %fusion.22.u_ref.ut_ref.alt_ref, f32[1024,1024]{1,0:T(8,128)} %fusion.22.u_ref.ut_ref.alt_ref, f32[1024,1024]{1,0:T(8,128)} %fusion.22.u_ref.ut_ref.alt_ref), custom_call_target="tpu_custom_call" | custom-call | tf_op jit(solution)/shard_map/pallas_call | solution.py:40
  42.8 5.9 %all-gather.6.cloned.1.call-done = f32[1,1024,1024]{2,1,0:T(8,128)} async-done(((f32[1,128,1024]{2,1,0:T(8,128)}), f32[1,1024,1024]{2,1,0:T(8,128)}) %all-gather.6.cloned.1.call-update) | async-done | bytes 4194320 | tf_op jit(solution)/shard_map/all_gather | solution.py:80
  48.8 54.7 %reduce-scatter.4.cloned.1.call-done = f32[128,1024]{1,0:T(8,128)} async-done(((f32[1024,1024]{1,0:T(8,128)}), f32[128,1024]{1,0:T(8,128)}) %reduce-scatter.4.cloned.1.call-update) | async-done | bytes 524304 | tf_op jit(solution)/shard_map/reduce_scatter | solution.py:84
  104.6 3.9 %fusion.55 = f32[1024,1024]{0,1:T(8,128)} fusion(f32[2,128,1024]{2,1,0:T(8,128)S(1)} %copy-done.3, s32[128]{0:T(128)S(1)} %iota_add_fusion, f32[2,128,1024]{2,1,0:T(8,128)S(1)} %copy-done.2), kind=kOutput, calls=%fused_computation.57 | convolution fusion | flops 805568512 | bytes 5243392 | tf_op jit(solution)/shard_map/dot_general | solution.py:16
  110.2 3.7 %fusion.7 = f32[128,1024]{1,0:T(8,128)S(1)} fusion(f32[128,1024]{1,0:T(8,128)S(1)} %convolution_subtract_fusion.2, f32[2,1024,1024]{2,1,0:T(8,128)} %param.5), kind=kOutput, calls=%fused_computation.7 | convolution fusion | flops 805306368 | bytes 5242880 | tf_op jit(solution)/shard_map/dot_general | solution.py:12
  117.9 3.8 %fusion.57 = f32[1024,1024]{1,0:T(8,128)} fusion(f32[128,1024]{1,0:T(8,128)S(1)} %fusion.7, f32[2,128,1024]{2,1,0:T(8,128)S(1)} %copy-done.2), kind=kOutput, calls=%fused_computation.59 | convolution fusion | flops 805306368 | bytes 5242880 | tf_op jit(solution)/shard_map/dot_general | solution.py:16
  121.7 20.6 %all-gather.4.cloned.1.call-done = f32[1024,1024]{1,0:T(8,128)} async-done(((f32[128,1024]{1,0:T(8,128)}), f32[1024,1024]{1,0:T(8,128)}) %all-gather.4.cloned.1.call-update) | async-done | bytes 4194320 | tf_op jit(solution)/shard_map/all_gather | solution.py:87
  142.2 10.4 %fusion.15 = f32[1024,1024]{1,0:T(8,128)S(1)} fusion(f32[1024,1024]{1,0:T(8,128)} %all-gather.4.cloned.1.call-done, f32[1024,1024]{1,0:T(8,128)} %fusion.57), kind=kOutput, calls=%fused_computation.15 | convolution fusion | flops 6444548096 | bytes 12582912 | tf_op jit(solution)/shard_map/dot_general | solution.py:16
  152.7 9.3 %fusion.2 = f32[1024,1024]{1,0:T(8,128)S(1)} fusion(f32[1024,1024]{1,0:T(8,128)S(1)} %fusion.15, f32[1024,1024]{0,1:T(8,128)S(1)} %copy-done.6, f32[2,1024,1024]{2,1,0:T(8,128)} %param.5), kind=kOutput, calls=%fused_computation.3 | convolution fusion | flops 6449790976 | bytes 16777216 | tf_op jit(solution)/shard_map/dot_general | solution.py:12
  161.9 10.1 %fusion.25.u_ref.ut_ref = f32[1024,1024]{1,0:T(8,128)} fusion(f32[1024,1024]{1,0:T(8,128)S(1)} %fusion.2, f32[2,1024,1024]{2,1,0:T(8,128)} %param.5), kind=kOutput, calls=%fused_computation.26 | convolution fusion | flops 6442450944 | bytes 12582912 | tf_op jit(solution)/shard_map/dot_general | solution.py:16
  173.0 1.7 add.31
  174.7 3.8 %fusion.61.alt_ref = f32[1024,1024]{1,0:T(8,128)} fusion(f32[2,128,1024]{2,1,0:T(8,128)S(1)} %add.31, f32[2,128,1024]{2,1,0:T(8,128)S(1)} %copy-done.2), kind=kOutput, calls=%fused_computation.63 | convolution fusion | flops 805306368 | bytes 5242880 | tf_op jit(solution)/shard_map/dot_general | solution.py:16
  178.5 12.5 %shard_map.38 = f32[2,1024,512]{2,1,0:T(8,128)} custom-call(s32[1]{0:T(128)} %bitcast.1.flag_ref, f32[1024,1024]{1,0:T(8,128)} %fusion.25.u_ref.ut_ref, f32[1024,1024]{1,0:T(8,128)} %fusion.25.u_ref.ut_ref, f32[1024,1024]{1,0:T(8,128)} %fusion.61.alt_ref), custom_call_target="tpu_custom_call" | custom-call | tf_op jit(solution)/shard_map/pallas_call | solution.py:40
  191.0 4.7 %slice_bitcast_fusion.1 = (f32[1024,512]{1,0:T(8,128)}, f32[1024,512]{1,0:T(8,128)}) fusion(f32[2,1024,512]{2,1,0:T(8,128)} %shard_map.38), kind=kLoop, calls=%fused_computation.32 | loop fusion | bytes 8388608 | tf_op jit(solution)/shard_map/squeeze | solution.py:103
  196.9 4.3 %convolution_subtract_fusion.1 = f32[128,1024]{1,0:T(8,128)} fusion(f32[1024,1024]{1,0:T(8,128)} %bitcast.86, f32[2,128,1024]{2,1,0:T(8,128)S(1)} %add.31, f32[2,128,1024]{2,1,0:T(8,128)S(1)} %copy-done.4), kind=kOutput, calls=%fused_computation.43 | convolution fusion | flops 805437440 | bytes 5767168 | tf_op jit(solution)/shard_map/dot_general | solution.py:12
  201.3 35.9 %reduce-scatter.8.cloned.1.call-done = f32[128,512]{1,0:T(8,128)} async-done(((f32[1024,512]{1,0:T(8,128)}), f32[128,512]{1,0:T(8,128)}) %reduce-scatter.8.cloned.1.call-update) | async-done | bytes 262160 | tf_op jit(solution)/shard_map/reduce_scatter | solution.py:103
  239.9 4.5 %fusion.40 = f32[1,128,1024]{2,1,0:T(8,128)} fusion(f32[128,1024]{1,0:T(8,128)} %convolution_subtract_fusion.1, f32[1024,1024]{1,0:T(8,128)} %all-gather.4.cloned.1.call-done, f32[128,1024]{1,0:T(8,128)S(1)} %fusion.7, f32[128,1024]{1,0:T(8,128)S(1)} %copy-done.5, f32[2,128,1024]{2,1,0:T(8,128)S(1)} %add.31, s32[128]{0:T(128)S(1)} %iota_add_fusion, ...), kind=kOutput, calls=%fused_computation.42 | convolution fusion | flops 806354944 | bytes 6816258 | tf_op jit(solution)/shard_map/dot_general | solution.py:12
  244.4 37.1 %reduce-scatter.6.cloned.1.call-done = f32[128,512]{1,0:T(8,128)} async-done(((f32[1024,512]{1,0:T(8,128)}), f32[128,512]{1,0:T(8,128)}) %reduce-scatter.6.cloned.1.call-update) | async-done | bytes 262160 | tf_op jit(solution)/shard_map/reduce_scatter | solution.py:103
  284.8 2.5 fusion.28
  287.3 6.6 %collective-permute-done.3 = f32[128,512]{1,0:T(8,128)S(1)} collective-permute-done((f32[128,512]{1,0:T(8,128)}, f32[128,512]{1,0:T(8,128)S(1)}, u32[]{:S(2)}, u32[]{:S(2)}) %collective-permute-start.3) | collective-permute-done | bytes 262176 | tf_op jit(solution)/shard_map/ppermute | solution.py:53
  (58 shorter events, 17.2 us)
Async XLA Ops:
  6.5 42.2 %all-gather.6.cloned.1.call-start = ((), (), s32[]{:S(2)}) async-start(), calls=%async_computation.7 | async-start | bytes 4718592 | tf_op jit(solution)/shard_map/all_gather | solution.py:80
  8.8 94.6 %reduce-scatter.4.cloned.1.call-start = ((), (), s32[]{:S(2)}) async-start(), calls=%async_computation.3 | async-start | bytes 4718592 | tf_op jit(solution)/shard_map/reduce_scatter | solution.py:84
  8.9 12.6 %slice-start = ((s8[8388608]{0:T(1024)(128)(4,1)}), s8[4194304]{0:T(1024)(128)(4,1)S(1)}, s32[]{:S(2)}) async-start(s8[8388608]{0:T(1024)(128)(4,1)} %bitcast.89), calls=%async_computation.8 | async-start | bytes 8388608
  12.2 9.3 %slice-start.1 = ((s8[8388608]{0:T(1024)(128)(4,1)}), s8[4194304]{0:T(1024)(128)(4,1)S(1)}, s32[]{:S(2)}) async-start(s8[8388608]{0:T(1024)(128)(4,1)} %bitcast.89), calls=%async_computation.9 | async-start | bytes 8388608
  42.8 61.7 %copy-start.2 = (f32[2,128,1024]{2,1,0:T(8,128)S(1)}, f32[2,128,1024]{2,1,0:T(8,128)}, u32[]{:S(2)}) copy-start(f32[2,128,1024]{2,1,0:T(8,128)} %param.3) | copy-start | bytes 3145732
  42.8 61.7 %copy-start.3 = (f32[2,128,1024]{2,1,0:T(8,128)S(1)}, f32[2,128,1024]{2,1,0:T(8,128)}, u32[]{:S(2)}) copy-start(f32[2,128,1024]{2,1,0:T(8,128)} %param.4) | copy-start | bytes 3145732
  48.7 93.5 %all-gather.4.cloned.1.call-start = ((), (), s32[]{:S(2)}) async-start(), calls=%async_computation.4 | async-start | bytes 4718592 | tf_op jit(solution)/shard_map/all_gather | solution.py:87
  103.4 5.0 %copy-start.5 = (f32[128,1024]{1,0:T(8,128)S(1)}, f32[128,1024]{1,0:T(8,128)}, u32[]{:S(2)}) copy-start(f32[128,1024]{1,0:T(8,128)} %reduce-scatter.4.cloned.1.call-done) | copy-start | bytes 1572868
  103.5 133.7 %reduce-scatter.8.cloned.1.call-start = ((), (), s32[]{:S(2)}) async-start(), calls=%async_computation.6 | async-start | bytes 2359296 | tf_op jit(solution)/shard_map/reduce_scatter | solution.py:103
  103.5 5.0 %collective-permute-start = (f32[128,1024]{1,0:T(8,128)}, f32[128,1024]{1,0:T(8,128)S(1)}, u32[]{:S(2)}, u32[]{:S(2)}) collective-permute-start(f32[128,1024]{1,0:T(8,128)} %reduce-scatter.4.cloned.1.call-done), channel_id=1, source_target_pairs={{24,16},{25,17},{26,18},{27,19},{28,20},{29,21},{30,22},{31,23}} | collective-permute-start | bytes 1572872 | tf_op jit(solution)/shard_map/ppermute | solution.py:88
  104.5 4.0 %copy-start.1 = (f32[1,1024,1024]{2,1,0:T(8,128)S(1)}, f32[1,1024,1024]{2,1,0:T(8,128)}, u32[]{:S(2)}) copy-start(f32[1,1024,1024]{2,1,0:T(8,128)} %all-gather.6.cloned.1.call-done) | copy-start | bytes 12582916
  114.9 57.1 %collective-permute-start.1 = (f32[2,128,1024]{2,1,0:T(8,128)}, f32[2,128,1024]{2,1,0:T(8,128)S(1)}, u32[]{:S(2)}, u32[]{:S(2)}) collective-permute-start(f32[2,128,1024]{2,1,0:T(8,128)} %pad_maximum_fusion), channel_id=1, source_target_pairs={{16,0},{17,1},{18,2},{19,3},{20,4},{21,5},{22,6},{23,7}} | collective-permute-start | bytes 3145736 | tf_op jit(solution)/shard_map/ppermute | solution.py:93
  116.2 56.8 %collective-permute-start.2 = (f32[2,128,1024]{2,1,0:T(8,128)}, f32[2,128,1024]{2,1,0:T(8,128)}, u32[]{:S(2)}, u32[]{:S(2)}) collective-permute-start(f32[2,128,1024]{2,1,0:T(8,128)} %pad_maximum_fusion), channel_id=1, source_target_pairs={{16,8},{17,9},{18,10},{19,11},{20,12},{21,13},{22,14},{23,15}} | collective-permute-start | bytes 3145736 | tf_op jit(solution)/shard_map/ppermute | solution.py:93
  142.2 10.4 %copy-start.6 = (f32[1024,1024]{0,1:T(8,128)S(1)}, f32[1024,1024]{0,1:T(8,128)}, u32[]{:S(2)}) copy-start(f32[1024,1024]{0,1:T(8,128)} %fusion.55) | copy-start | bytes 12582916
  195.7 1.2 copy-start.4
  195.7 85.8 %reduce-scatter.6.cloned.1.call-start = ((), (), s32[]{:S(2)}) async-start(), calls=%async_computation.5 | async-start | bytes 2359296 | tf_op jit(solution)/shard_map/reduce_scatter | solution.py:103
  237.1 47.6 %copy-start.10 = (f32[128,512]{1,0:T(8,128)S(1)}, f32[128,512]{1,0:T(8,128)}, u32[]{:S(2)}) copy-start(f32[128,512]{1,0:T(8,128)} %reduce-scatter.8.cloned.1.call-done) | copy-start | bytes 786436
  237.1 47.6 %collective-permute-start.5 = (f32[128,512]{1,0:T(8,128)}, f32[128,512]{1,0:T(8,128)}, u32[]{:S(2)}, u32[]{:S(2)}) collective-permute-start(f32[128,512]{1,0:T(8,128)} %reduce-scatter.8.cloned.1.call-done), channel_id=1, source_target_pairs={{16,0},{17,1},{18,2},{19,3},{20,4},{21,5},{22,6},{23,7}} | collective-permute-start | bytes 786440 | tf_op jit(solution)/shard_map/ppermute | solution.py:53
  238.5 46.2 %collective-permute-start.6 = (f32[128,512]{1,0:T(8,128)}, f32[128,512]{1,0:T(8,128)}, u32[]{:S(2)}, u32[]{:S(2)}) collective-permute-start(f32[128,512]{1,0:T(8,128)} %reduce-scatter.8.cloned.1.call-done), channel_id=1, source_target_pairs={{16,8},{17,9},{18,10},{19,11},{20,12},{21,13},{22,14},{23,15}} | collective-permute-start | bytes 786440 | tf_op jit(solution)/shard_map/ppermute | solution.py:53
  281.5 12.5 %copy-start = (f32[1024,1024]{1,0:T(8,128)S(1)}, f32[1024,1024]{1,0:T(8,128)}, u32[]{:S(2)}) copy-start(f32[1024,1024]{1,0:T(8,128)} %all-gather.4.cloned.1.call-done) | copy-start | bytes 12582916
  281.5 12.5 %copy-start.9 = (f32[128,512]{1,0:T(8,128)S(1)}, f32[128,512]{1,0:T(8,128)}, u32[]{:S(2)}) copy-start(f32[128,512]{1,0:T(8,128)} %reduce-scatter.6.cloned.1.call-done) | copy-start | bytes 786436
  281.5 12.5 %collective-permute-start.3 = (f32[128,512]{1,0:T(8,128)}, f32[128,512]{1,0:T(8,128)S(1)}, u32[]{:S(2)}, u32[]{:S(2)}) collective-permute-start(f32[128,512]{1,0:T(8,128)} %reduce-scatter.6.cloned.1.call-done), channel_id=1, source_target_pairs={{16,0},{17,1},{18,2},{19,3},{20,4},{21,5},{22,6},{23,7}} | collective-permute-start | bytes 786440 | tf_op jit(solution)/shard_map/ppermute | solution.py:53
  283.1 10.9 %collective-permute-start.4 = (f32[128,512]{1,0:T(8,128)}, f32[128,512]{1,0:T(8,128)S(1)}, u32[]{:S(2)}, u32[]{:S(2)}) collective-permute-start(f32[128,512]{1,0:T(8,128)} %reduce-scatter.6.cloned.1.call-done), channel_id=1, source_target_pairs={{16,8},{17,9},{18,10},{19,11},{20,12},{21,13},{22,14},{23,15}} | collective-permute-start | bytes 786440 | tf_op jit(solution)/shard_map/ppermute | solution.py:53
  284.7 10.2 %copy-start.7 = (f32[1,128,1024]{2,1,0:T(8,128)S(1)}, f32[1,128,1024]{2,1,0:T(8,128)}, u32[]{:S(2)}) copy-start(f32[1,128,1024]{2,1,0:T(8,128)} %fusion.40) | copy-start | bytes 1572868
  (1 other events, 1.0 us)
Sparse Core Ops, SparseCore 0:
  9.2 39.4 all-gather.5
  52.0 51.3 reduce-scatter.3
  105.5 36.6 all-gather.3
  195.8 41.2 reduce-scatter.7
  240.3 41.1 reduce-scatter.5
